TPU v7x, 256 devices: a whole 4x4x8 slice. The times are simulated.
256 devices in a mesh: dp: 4 (over z_lo, core), cp: 16 (over y, z_hi), tp: 4 (over x).
Axes of the slice: x: 4, y: 4, z: 8 (z_hi: 4, z_lo: 2; z = z_hi * 2 + z_lo), core: 2. Of those that a mesh axis runs over, the one named last changes fastest.
Arguments:
- hidden: bfloat16 [4, 2048, 8192], P('dp', 'cp'), may hold values from -6 to 6
- query: bfloat16 [4, 2048, 8192], P('dp', 'cp', 'tp'), may hold values from -360 to 360
- grad_out: bfloat16 [4, 2048, 8192], P('dp', 'cp', 'tp'), may hold values from -6 to 6
- k_weight: bfloat16 [8192, 1024], P('dp', 'tp'), may hold values from -0.0625 to 0.0625
- v_weight: bfloat16 [8192, 1024], P('dp', 'tp'), may hold values from -0.0625 to 0.0625
- doc_starts: int32 [4, 4], P('dp'), may hold values from 0 to 2047, as said below
Outputs:
- attn_out: bfloat16 [4, 2048, 8192], P('dp', 'cp', 'tp')
- query_grad: bfloat16 [4, 2048, 8192], P('dp', 'cp', 'tp')
- k_weight_grad: float32 [8192, 1024], P(('dp', 'cp'), 'tp')
- v_weight_grad: float32 [8192, 1024], P(('dp', 'cp'), 'tp')
Inputs may be any that keep to these rules, and one draw needn't show every extreme that they name: `doc_starts`: in each sequence the starts strictly increase and the first is 0.
All inputs are finite; a program needn't handle non-finite values.
Results may differ from a plain program's by a relative error of at most 0.04.
The roundings to bfloat16 on the way count: a program that leaves them out, or rounds other values in their place, can miss the bound.
Values may be sent and summed in bfloat16 or wider, within the bound.
No kernel may reach another device: no remote copies, remote signals or barrier semaphores. Data moves between devices by JAX's collectives and lax.ppermute only.
A program may use at most 128 MiB of HBM per device.

v0:
```python
import jax
import jax.numpy as jnp
from jax import lax
from jax.sharding import PartitionSpec as P

DH = 128
NEG_BIG = -1e30


def place(rows, tok_rows, seq_rows):
    stretch = rows // tok_rows
    within = rows % tok_rows
    half_rows = tok_rows // 2
    return jnp.where(
        within < half_rows,
        stretch * half_rows + within,
        seq_rows - (stretch + 1) * half_rows + within - half_rows,
    )


def doc_index(positions, starts):
    return jnp.sum((starts[None, :] <= positions[:, None]).astype(jnp.int32), axis=1) - 1


def on_device(hidden, query, grad_out, k_weight, v_weight, doc_starts):
    inputs = hidden[0]
    tok_rows, width = inputs.shape
    cp_count = lax.axis_size("cp")
    dp_count = lax.axis_size("dp")
    seq_rows = tok_rows * cp_count
    score_scale = DH ** (-0.5)
    kv_width = k_weight.shape[1]
    kv_heads = kv_width // DH
    per_group = query.shape[2] // DH // kv_heads
    starts = doc_starts[0]
    blk = width // (dp_count * cp_count)
    cols = inputs.reshape(tok_rows, dp_count, cp_count, blk).transpose(2, 0, 1, 3)
    cols = lax.all_to_all(cols, "cp", 0, 0, tiled=True)
    both_w = jnp.concatenate([k_weight, v_weight], axis=1)
    both_w = lax.all_gather(both_w, "dp", axis=0, tiled=True)
    kv = jnp.dot(inputs, both_w, preferred_element_type=jnp.float32).astype(jnp.bfloat16)
    kv_all = lax.all_gather(kv, "cp", axis=0, tiled=True)
    key_heads = kv_all[:, :kv_width].reshape(seq_rows, kv_heads, DH)
    value_heads = kv_all[:, kv_width:].reshape(seq_rows, kv_heads, DH)
    own_rows = lax.axis_index("cp") * tok_rows + jnp.arange(tok_rows, dtype=jnp.int32)
    own_place = place(own_rows, tok_rows, seq_rows)
    own_doc = doc_index(own_place, starts)
    key_place = place(jnp.arange(seq_rows, dtype=jnp.int32), tok_rows, seq_rows)
    key_doc = doc_index(key_place, starts)
    allowed = (key_place[None, :] <= own_place[:, None]) & (key_doc[None, :] == own_doc[:, None])
    queries = query[0].reshape(tok_rows, kv_heads, per_group, DH)
    upstream = grad_out[0].reshape(tok_rows, kv_heads, per_group, DH)
    scores = (
        jnp.einsum("qgid,kgd->giqk", queries, key_heads, preferred_element_type=jnp.float32)
        * score_scale
    )
    scores = jnp.where(allowed, scores, NEG_BIG)
    top_score = jnp.max(scores, axis=-1)
    expos = jnp.where(allowed, jnp.exp(scores - top_score[..., None]), 0.0)
    log_total = top_score + jnp.log(jnp.sum(expos, axis=-1))
    weights = jnp.where(allowed, jnp.exp(scores - log_total[..., None]), 0.0)
    weights_bf = weights.astype(jnp.bfloat16)
    out_rows = jnp.einsum(
        "giqk,kgd->qgid", weights_bf, value_heads, preferred_element_type=jnp.float32
    ).astype(jnp.bfloat16)
    delta = jnp.transpose(
        jnp.sum(upstream.astype(jnp.float32) * out_rows.astype(jnp.float32), axis=-1), (1, 2, 0)
    )
    prob_grads = jnp.einsum(
        "qgid,kgd->giqk", upstream, value_heads, preferred_element_type=jnp.float32
    )
    score_grads = (weights * (prob_grads - delta[..., None])).astype(jnp.bfloat16)
    query_acc = (
        jnp.einsum("giqk,kgd->qgid", score_grads, key_heads, preferred_element_type=jnp.float32)
        * score_scale
    )
    key_term = (
        jnp.einsum("giqk,qgid->kgd", score_grads, queries, preferred_element_type=jnp.float32)
        * score_scale
    )
    value_term = jnp.einsum(
        "giqk,qgid->kgd", weights_bf, upstream, preferred_element_type=jnp.float32
    )
    both_terms = jnp.concatenate(
        [key_term.reshape(seq_rows, kv_width), value_term.reshape(seq_rows, kv_width)], axis=1
    ).astype(jnp.bfloat16)
    both_grads = lax.psum(both_terms, "cp")
    grads = both_grads.reshape(cp_count, tok_rows, 2 * kv_width)
    partial = jnp.einsum("ctjb,ctn->jbn", cols, grads, preferred_element_type=jnp.float32)
    result = lax.psum_scatter(partial, "dp", scatter_dimension=0, tiled=True)[0]
    attn_rows = out_rows.reshape(1, tok_rows, kv_heads * per_group * DH)
    query_rows = query_acc.astype(jnp.bfloat16).reshape(1, tok_rows, kv_heads * per_group * DH)
    return (attn_rows, query_rows, result[:, :kv_width], result[:, kv_width:])


def solution(mesh):
    placed = (
        P("dp", "cp", None),
        P("dp", "cp", "tp"),
        P("dp", "cp", "tp"),
        P("dp", "tp"),
        P("dp", "tp"),
        P("dp", None),
    )
    return jax.shard_map(
        on_device,
        mesh=mesh,
        in_specs=placed,
        out_specs=(
            P("dp", "cp", "tp"),
            P("dp", "cp", "tp"),
            P(("dp", "cp"), "tp"),
            P(("dp", "cp"), "tp"),
        ),
        check_vma=False,
    )
```

profile of v0, /device:TPU:1, one launch (start us, length us, event | category | flops | bytes accessed | tf_op | source)
XLA Modules:
  0.0 460.0 jit_solution(11077758612200397458)
XLA Ops:
  7.2 3.1 pad_maximum_fusion
  10.3 88.3 %all-gather.3.cloned.1.call-done = bf16[8192,512]{1,0:T(8,128)(2,1)} async-done(((bf16[2048,512]{1,0:T(8,128)(2,1)}), bf16[8192,512]{1,0:T(8,128)(2,1)}) %all-gather.3.cloned.1.call-update) | async-done | bytes 8388624 | tf_op jit(solution)/shard_map/all_gather | solution.py:40
  98.7 7.0 %fusion.18 = bf16[128,512]{0,1:T(8,128)(2,1)} fusion(bf16[8192,512]{1,0:T(8,128)(2,1)} %all-gather.3.cloned.1.call-done, bf16[1,128,8192]{2,1,0:T(8,128)(2,1)} %param.6), kind=kOutput, calls=%fused_computation.24 | convolution fusion | flops 1073807360 | bytes 10616832 | tf_op jit(solution)/shard_map/dot_general | solution.py:41
  105.7 3.3 copy.76
  109.0 2.6 copy.77
  111.6 8.4 %all-to-all-start = ((bf16[16,128,4,128]{3,1,2,0:T(8,128)(2,1)}), bf16[16,128,4,128]{3,1,2,0:T(8,128)(2,1)}, u32[]{:S(2)}, u32[]{:S(2)}) async-start(bf16[16,128,4,128]{3,1,2,0:T(8,128)(2,1)} %copy.77), calls=%async_computation | async-start | bytes 4194304 | tf_op jit(solution)/shard_map/all_to_all | solution.py:38
  121.9 1.3 compare_and_fusion
  123.2 66.3 %all-gather.5.cloned.1.call-done = bf16[2048,512]{0,1:T(8,128)(2,1)} async-done(((bf16[128,512]{0,1:T(8,128)(2,1)}), bf16[2048,512]{0,1:T(8,128)(2,1)}) %all-gather.5.cloned.1.call-update) | async-done | bytes 2097168 | tf_op jit(solution)/shard_map/all_gather | solution.py:42
  189.5 2.7 fusion.39
  192.2 2.6 fusion.3
  194.8 4.0 select_reduce_fusion
  198.8 1.7 copy-done
  200.6 8.2 %fusion.6 = bf16[2,2048,128]{1,2,0:T(8,128)(2,1)S(1)} fusion(bf16[128,2,8,128]{0,3,2,1:T(8,128)(2,1)S(1)} %bitcast.117, f32[2,2048,128,8]{2,1,3,0:T(8,128)} %copy-done, f32[2,8,128]{2,1,0:T(8,128)S(1)} %log_add_fusion, pred[128,2048]{0,1:T(8,128)(4,1)S(1)} %compare_and_fusion), kind=kOutput, calls=%fused_computation.12 | convolution fusion | flops 1095237632 | bytes 18620416 | tf_op jit(solution)/shard_map/giqk,qgid->kgd/dot_general | solution.py:81
  210.1 11.1 %multiply_reduce_fusion = (f32[128,2,8]{0,2,1:T(8,128)S(1)}, bf16[2,128,8,128]{3,1,2,0:T(8,128)(2,1)}) fusion(bf16[128,2,8,128]{0,3,2,1:T(8,128)(2,1)S(1)} %bitcast.118, bf16[2048,2,128,1]{0,2,3,1:T(8,128)(2,1)} %bitcast.114, f32[2,2048,128,8]{2,1,3,0:T(8,128)} %copy-done, f32[2,8,128]{2,1,0:T(8,128)S(1)} %log_add_fusion, ...), kind=kOutput, calls=%fused_computation.25 | convolution fusion | flops 1096022016 | bytes 19152896 | tf_op jit(solution)/shard_map/giqk,kgd->qgid/dot_general | solution.py:63
  221.3 9.3 %fusion.1 = bf16[2,8,128,2048]{2,3,1,0:T(8,128)(2,1)S(1)} fusion(f32[2,2048,128,8]{2,1,3,0:T(8,128)} %copy-done, f32[2,8,128]{2,1,0:T(8,128)S(1)} %bitcast.123, f32[2,8,128]{2,1,0:T(8,128)S(1)} %log_add_fusion, pred[128,2048]{0,1:T(8,128)(4,1)S(1)} %compare_and_fusion, bf16[2048,2,128,1]{0,2,3,1:T(8,128)(2,1)S(1)} %bitcast.115, ...), kind=kOutput, calls=%fused_computation.2 | convolution fusion | flops 1103101952 | bytes 27017216 | tf_op jit(solution)/shard_map/qgid,kgd->giqk/dot_general | solution.py:69
  230.5 3.2 copy-done.1
  233.7 2.8 fusion.5
  236.6 1.3 copy.73
  237.9 1.7 pad_maximum_fusion.1
  239.6 2.4 copy.75
  242.1 174.2 %all-reduce.2.cloned.1.call-done = bf16[16,128,512]{1,2,0:T(8,128)(2,1)} async-done(((bf16[16,128,512]{1,2,0:T(8,128)(2,1)}), bf16[16,128,512]{1,2,0:T(8,128)(2,1)}) %all-reduce.2.cloned.1.call-update) | async-done | bytes 2097168 | tf_op jit(solution)/shard_map/psum | solution.py:87
  416.3 4.4 fusion.11
  420.8 4.7 %fusion.14 = bf16[2,128,8,128]{3,1,2,0:T(8,128)(2,1)S(1)} fusion(bf16[2048,2,128,1]{0,2,3,1:T(8,128)(2,1)S(1)} %bitcast.106, bf16[2,8,128,2048]{2,3,1,0:T(8,128)(2,1)} %copy-done.1), kind=kOutput, calls=%fused_computation.21 | convolution fusion | flops 1074266112 | bytes 9961472 | tf_op jit(solution)/shard_map/giqk,kgd->qgid/dot_general | solution.py:74
  427.5 23.4 %reduce-scatter.2.cloned.1.call-done = f32[1,128,512]{1,2,0:T(8,128)} async-done(((f32[4,128,512]{1,2,0:T(8,128)}), f32[1,128,512]{1,2,0:T(8,128)}) %reduce-scatter.2.cloned.1.call-update) | async-done | bytes 262160 | tf_op jit(solution)/shard_map/reduce_scatter | solution.py:90
  (38 shorter events, 7.8 us)
Async XLA Ops:
  7.2 91.5 %all-gather.3.cloned.1.call-start = ((), (), s32[]{:S(2)}) async-start(), calls=%async_computation.2 | async-start | bytes 10485760 | tf_op jit(solution)/shard_map/all_gather | solution.py:40
  10.3 179.2 %all-gather.5.cloned.1.call-start = ((), (), s32[]{:S(2)}) async-start(), calls=%async_computation.3 | async-start | bytes 2228224 | tf_op jit(solution)/shard_map/all_gather | solution.py:42
  105.7 14.6 %copy-start.3 = (bf16[1,128,2048]{2,1,0:T(8,128)(2,1)S(1)}, bf16[1,128,2048]{2,1,0:T(8,128)(2,1)}, u32[]{:S(2)}) copy-start(bf16[1,128,2048]{2,1,0:T(8,128)(2,1)} %param.7) | copy-start | bytes 1572868
  105.7 14.9 %copy-start.4 = (bf16[1,128,2048]{2,1,0:T(8,128)(2,1)S(1)}, bf16[1,128,2048]{2,1,0:T(8,128)(2,1)}, u32[]{:S(2)}) copy-start(bf16[1,128,2048]{2,1,0:T(8,128)(2,1)} %param.8) | copy-start | bytes 1572868
  105.7 16.0 %copy-start.7 = (s32[1,4]{1,0:T(1,128)S(1)}, s32[1,4]{1,0:T(1,128)}, u32[]{:S(2)}) copy-start(s32[1,4]{1,0:T(1,128)} %param.11) | copy-start | bytes 52
  111.6 130.4 %all-to-all-start = ((bf16[16,128,4,128]{3,1,2,0:T(8,128)(2,1)}), bf16[16,128,4,128]{3,1,2,0:T(8,128)(2,1)}, u32[]{:S(2)}, u32[]{:S(2)}) async-start(bf16[16,128,4,128]{3,1,2,0:T(8,128)(2,1)} %copy.77), calls=%async_computation | async-start | bytes 4194304 | tf_op jit(solution)/shard_map/all_to_all | solution.py:38
  120.1 296.2 %all-reduce.2.cloned.1.call-start = ((), (), s32[]{:S(2)}) async-start(), calls=%async_computation.4 | async-start | bytes 4194304 | tf_op jit(solution)/shard_map/psum | solution.py:87
  194.8 5.7 %copy-start = (f32[2,2048,128,8]{2,1,3,0:T(8,128)}, f32[2,2048,128,8]{2,1,3,0:T(8,128)S(1)}, u32[]{:S(2)}) copy-start(f32[2,2048,128,8]{2,1,3,0:T(8,128)S(1)} %get-tuple-element.25) | copy-start | bytes 50331652
  194.8 5.7 %copy-start.6 = (bf16[1,128,2048]{1,2,0:T(8,128)(2,1)S(1)}, bf16[1,128,2048]{1,2,0:T(8,128)(2,1)}, u32[]{:S(2)}) copy-start(bf16[1,128,2048]{1,2,0:T(8,128)(2,1)} %copy.66) | copy-start | bytes 1572868
  210.1 11.1 %copy-start.2 = (bf16[2048,256]{0,1:T(8,128)(2,1)S(1)}, bf16[2048,256]{0,1:T(8,128)(2,1)}, u32[]{:S(2)}) copy-start(bf16[2048,256]{0,1:T(8,128)(2,1)} %get-tuple-element.21) | copy-start | bytes 3145732
  230.5 3.2 copy-start.1
  242.0 208.9 %reduce-scatter.2.cloned.1.call-start = ((), (), s32[]{:S(2)}) async-start(), calls=%async_computation.5 | async-start | bytes 1310720 | tf_op jit(solution)/shard_map/reduce_scatter | solution.py:90
  420.8 5.7 %copy-start.5 = (bf16[2,128,8,128]{3,1,2,0:T(8,128)(2,1)S(1)}, bf16[2,128,8,128]{3,1,2,0:T(8,128)(2,1)}, u32[]{:S(2)}) copy-start(bf16[2,128,8,128]{3,1,2,0:T(8,128)(2,1)} %get-tuple-element.27) | copy-start | bytes 1572868
Sparse Core Ops, SparseCore 0:
  10.4 88.2 all-gather.2
  105.8 83.6 all-gather.4
  242.2 174.1 all-reduce.1
  420.9 30.0 reduce-scatter.1
where the time goes:
time: 460 us
  waiting for transfers between devices  352 us (77%)
  matrix products  50.2 us (11%)
  local copies, waits for them, and re-layouts  24.5 us (5%)
  between operations  14 us (3%)
  other arithmetic  10.3 us (2%)
  starting transfers between devices  8.78 us (2%)
    psum x1, waiting for transfers between devices, on_device(): both_grads = lax.psum(both_terms, 'cp')  174 us
    all_gather x1, waiting for transfers between devices, on_device(): both_w = lax.all_gather(both_w, 'dp', axis=0, tiled=True)  88.3 us
    all_gather x1, waiting for transfers between devices, on_device(): kv_all = lax.all_gather(kv, 'cp', axis=0, tiled=True)  66.3 us
    reduce_scatter x1, waiting for transfers between devices, on_device(): result = lax.psum_scatter(partial, 'dp', scatter_dimension=0, tiled=True)[0]  23.4 us
    unnamed x22, local copies, waits for them, and re-layouts  12.8 us
    dot_general x1, matrix products, on_device(): jnp.einsum('giqk,kgd->qgid', weights_bf, value_heads, preferred_element_t...  11.1 us
    dot_general x1, matrix products, on_device(): jnp.einsum('qgid,kgd->giqk', upstream, value_heads, preferred_element_typ...  9.25 us
  transfers between devices with their start and end apart: 5, of which 4 were waited for; matrix products, arithmetic and copies ran while one was open for 14% of the time, Pallas kernels for 0%

commit v1 on v0

--- a/solution.py
+++ b/solution.py
@@ -2,9 +2,11 @@
 import jax.numpy as jnp
 from jax import lax
 from jax.sharding import PartitionSpec as P
+from jax.lax import all_gather
 
 DH = 128
 NEG_BIG = -1e30
+guide_ends = lambda mat: all_gather(mat, axis_name="cp").sum(axis=0)
 
 
 def place(rows, tok_rows, seq_rows):
@@ -84,7 +86,7 @@
     both_terms = jnp.concatenate(
         [key_term.reshape(seq_rows, kv_width), value_term.reshape(seq_rows, kv_width)], axis=1
     ).astype(jnp.bfloat16)
-    both_grads = lax.psum(both_terms, "cp")
+    both_grads = guide_ends(both_terms)
     grads = both_grads.reshape(cp_count, tok_rows, 2 * kv_width)
     partial = jnp.einsum("ctjb,ctn->jbn", cols, grads, preferred_element_type=jnp.float32)
     result = lax.psum_scatter(partial, "dp", scatter_dimension=0, tiled=True)[0]

time: 460 us -> 685 us (1.49)
  waiting for transfers between devices: 352 us -> 565 us
  other arithmetic: 10.3 us -> 24.3 us
    all_gather x0 -> x1, waiting for transfers between devices: none -> 402 us  [guide_ends = lambda mat: all_gather(mat, axis_name='cp').sum(axis=0)]
    psum x1 -> x0, waiting for transfers between devices: 174 us -> none  [on_device(): both_grads = lax.psum(both_terms, 'cp')]
    reduce_sum x0 -> x1, other arithmetic: none -> 13 us  [guide_ends = lambda mat: all_gather(mat, axis_name='cp').sum(axis=0)]
    reduce_scatter x1, waiting for transfers between devices: 23.4 us -> 15.4 us  [on_device(): result = lax.psum_scatter(partial, 'dp', scatter_dimension=0, tiled=True)[0]]
    all_gather x1, waiting for transfers between devices: 66.3 us -> 59.1 us  [on_device(): kv_all = lax.all_gather(kv, 'cp', axis=0, tiled=True)]
  transfers between devices with their start and end apart: 5 -> 5, of which waited for: 4 -> 4; matrix products, arithmetic and copies ran while one was open for 14% -> 4% of each run, Pallas kernels for 0% -> 0%
where the time goes in v1:
time: 685 us; the launch traced here: 684 us
  waiting for transfers between devices  565 us (82%)
  matrix products  54.9 us (8%)
  other arithmetic  24.3 us (4%)
  local copies, waits for them, and re-layouts  20.3 us (3%)
  between operations  13.9 us (2%)
    all_gather x1, waiting for transfers between devices, guide_ends = lambda mat: all_gather(mat, axis_name='cp').sum(axis=0)  402 us
    all_gather x1, waiting for transfers between devices, on_device(): both_w = lax.all_gather(both_w, 'dp', axis=0, tiled=True)  88.3 us
    all_gather x1, waiting for transfers between devices, on_device(): kv_all = lax.all_gather(kv, 'cp', axis=0, tiled=True)  59.1 us
    reduce_scatter x1, waiting for transfers between devices, on_device(): result = lax.psum_scatter(partial, 'dp', scatter_dimension=0, tiled=True)[0]  15.4 us
  transfers between devices with their start and end apart: 5, of which 4 were waited for; matrix products, arithmetic and copies ran while one was open for 4% of the time, Pallas kernels for 0%

profile of v1, /device:TPU:1, one launch (start us, length us, event | category | flops | bytes accessed | tf_op | source)
XLA Modules:
  0.0 684.3 jit_solution(2530637190831205520)
XLA Ops:
  7.2 3.0 pad_maximum_fusion
  10.4 88.3 %all-gather.4.cloned.1.call-done = bf16[8192,512]{1,0:T(8,128)(2,1)} async-done(((bf16[2048,512]{1,0:T(8,128)(2,1)}), bf16[8192,512]{1,0:T(8,128)(2,1)}) %all-gather.4.cloned.1.call-update) | async-done | bytes 8388624 | tf_op jit(solution)/shard_map/all_gather | solution.py:42
  98.7 7.0 %fusion.13 = bf16[128,512]{0,1:T(8,128)(2,1)} fusion(bf16[8192,512]{1,0:T(8,128)(2,1)} %all-gather.4.cloned.1.call-done, bf16[1,128,8192]{2,1,0:T(8,128)(2,1)} %param.6), kind=kOutput, calls=%fused_computation.22 | convolution fusion | flops 1073807360 | bytes 10616832 | tf_op jit(solution)/shard_map/dot_general | solution.py:43
  106.8 1.3 compare_and_fusion
  108.1 59.1 %all-gather.6.cloned.1.call-done = bf16[2048,512]{0,1:T(8,128)(2,1)} async-done(((bf16[128,512]{0,1:T(8,128)(2,1)}), bf16[2048,512]{0,1:T(8,128)(2,1)}) %all-gather.6.cloned.1.call-update) | async-done | bytes 2097168 | tf_op jit(solution)/shard_map/all_gather | solution.py:44
  167.2 2.7 fusion.34
  169.9 2.6 fusion.3
  172.5 4.0 select_reduce_fusion
  176.5 1.7 copy-done
  178.2 9.3 %fusion.6 = bf16[2,2048,128]{1,2,0:T(8,128)(2,1)} fusion(bf16[128,2,8,128]{0,3,2,1:T(8,128)(2,1)S(1)} %bitcast.115, f32[2,2048,128,8]{2,1,3,0:T(8,128)} %copy-done, f32[2,8,128]{2,1,0:T(8,128)S(1)} %log_add_fusion, pred[128,2048]{0,1:T(8,128)(4,1)S(1)} %compare_and_fusion), kind=kOutput, calls=%fused_computation.12 | convolution fusion | flops 1095237632 | bytes 18620416 | tf_op jit(solution)/shard_map/giqk,qgid->kgd/dot_general | solution.py:83
  187.5 11.2 %multiply_reduce_fusion = (f32[128,2,8]{0,2,1:T(8,128)S(1)}, bf16[2,128,8,128]{3,1,2,0:T(8,128)(2,1)}) fusion(bf16[128,2,8,128]{0,3,2,1:T(8,128)(2,1)S(1)} %bitcast.116, bf16[2048,2,128,1]{0,2,3,1:T(8,128)(2,1)} %bitcast.112, f32[2,2048,128,8]{2,1,3,0:T(8,128)} %copy-done, f32[2,8,128]{2,1,0:T(8,128)S(1)} %log_add_fusion, ...), kind=kOutput, calls=%fused_computation.23 | convolution fusion | flops 1096022016 | bytes 19152896 | tf_op jit(solution)/shard_map/giqk,kgd->qgid/dot_general | solution.py:65
  198.7 9.4 %fusion.1 = bf16[2,8,128,2048]{2,3,1,0:T(8,128)(2,1)} fusion(f32[2,2048,128,8]{2,1,3,0:T(8,128)S(1)} %copy-done.1, f32[2,8,128]{2,1,0:T(8,128)S(1)} %bitcast.121, f32[2,8,128]{2,1,0:T(8,128)S(1)} %log_add_fusion, pred[128,2048]{0,1:T(8,128)(4,1)S(1)} %compare_and_fusion, bf16[2048,2,128,1]{0,2,3,1:T(8,128)(2,1)} %bitcast.113, ...), kind=kOutput, calls=%fused_computation.2 | convolution fusion | flops 1103101952 | bytes 27017216 | tf_op jit(solution)/shard_map/qgid,kgd->giqk/dot_general | solution.py:71
  208.1 2.3 copy.74
  210.4 6.2 fusion.5
  217.2 2.7 pad_maximum_fusion.1
  219.9 4.1 copy.77
  224.0 3.9 copy.78
  227.9 5.6 all-to-all-start
  233.5 402.1 %all-gather.8.cloned.1.call-done = bf16[16,2048,512]{2,1,0:T(8,128)(2,1)} async-done(((bf16[1,2048,512]{2,1,0:T(8,128)(2,1)}), bf16[16,2048,512]{2,1,0:T(8,128)(2,1)}) %all-gather.8.cloned.1.call-update) | async-done | bytes 33554448 | tf_op jit(solution)/shard_map/all_gather | solution.py:9
  635.6 13.0 %reduce_sum.52 = bf16[2048,512]{1,0:T(8,128)(2,1)} reduce(bf16[16,2048,512]{2,1,0:T(8,128)(2,1)} %all-gather.8.cloned.1.call-done, bf16[]{:T(256)} %constant.84.clone.1), dimensions={0}, to_apply=%region_5.6 | reduce | flops 15728640 | bytes 35651584 | tf_op jit(solution)/shard_map/reduce_sum | solution.py:9
  648.6 4.5 convolution_bitcast_fusion.2
  653.1 1.0 copy.81
  654.2 4.7 fusion.9
  659.9 15.4 %reduce-scatter.2.cloned.1.call-done = f32[1,128,512]{1,2,0:T(8,128)} async-done(((f32[4,128,512]{1,2,0:T(8,128)}), f32[1,128,512]{1,2,0:T(8,128)}) %reduce-scatter.2.cloned.1.call-update) | async-done | bytes 262160 | tf_op jit(solution)/shard_map/reduce_scatter | solution.py:92
  (34 shorter events, 5.2 us)
Async XLA Ops:
  7.2 91.5 %all-gather.4.cloned.1.call-start = ((), (), s32[]{:S(2)}) async-start(), calls=%async_computation.2 | async-start | bytes 10485760 | tf_op jit(solution)/shard_map/all_gather | solution.py:42
  10.3 95.6 %copy-start.2 = (bf16[1,128,2048]{2,1,0:T(8,128)(2,1)S(1)}, bf16[1,128,2048]{2,1,0:T(8,128)(2,1)}, u32[]{:S(2)}) copy-start(bf16[1,128,2048]{2,1,0:T(8,128)(2,1)} %param.8) | copy-start | bytes 1572868
  10.3 95.9 %copy-start.3 = (bf16[1,128,2048]{2,1,0:T(8,128)(2,1)S(1)}, bf16[1,128,2048]{2,1,0:T(8,128)(2,1)}, u32[]{:S(2)}) copy-start(bf16[1,128,2048]{2,1,0:T(8,128)(2,1)} %param.7) | copy-start | bytes 1572868
  10.3 96.2 %copy-start.5 = (s32[1,4]{1,0:T(1,128)S(1)}, s32[1,4]{1,0:T(1,128)}, u32[]{:S(2)}) copy-start(s32[1,4]{1,0:T(1,128)} %param.11) | copy-start | bytes 52
  10.3 156.9 %all-gather.6.cloned.1.call-start = ((), (), s32[]{:S(2)}) async-start(), calls=%async_computation.3 | async-start | bytes 2228224 | tf_op jit(solution)/shard_map/all_gather | solution.py:44
  105.7 529.9 %all-gather.8.cloned.1.call-start = ((), (), s32[]{:S(2)}) async-start(), calls=%async_computation.4 | async-start | bytes 35651584 | tf_op jit(solution)/shard_map/all_gather | solution.py:9
  172.5 5.7 copy-start
  187.5 11.2 %copy-start.1 = (f32[2,2048,128,8]{2,1,3,0:T(8,128)S(1)}, f32[2,2048,128,8]{2,1,3,0:T(8,128)}, u32[]{:S(2)}) copy-start(f32[2,2048,128,8]{2,1,3,0:T(8,128)} %copy-done) | copy-start | bytes 50331652
  227.9 420.7 %all-to-all-start = ((bf16[16,128,4,128]{3,1,2,0:T(8,128)(2,1)}), bf16[16,128,4,128]{3,1,2,0:T(8,128)(2,1)}, u32[]{:S(2)}, u32[]{:S(2)}) async-start(bf16[16,128,4,128]{3,1,2,0:T(8,128)(2,1)} %copy.78), calls=%async_computation | async-start | bytes 4194304 | tf_op jit(solution)/shard_map/all_to_all | solution.py:40
  233.5 441.8 %reduce-scatter.2.cloned.1.call-start = ((), (), s32[]{:S(2)}) async-start(), calls=%async_computation.5 | async-start | bytes 1310720 | tf_op jit(solution)/shard_map/reduce_scatter | solution.py:92
  648.6 4.6 copy-start.4
Sparse Core Ops, SparseCore 0:
  10.4 88.2 all-gather.3
  105.8 61.3 all-gather.5
  220.0 415.5 all-gather.7
  653.3 21.9 reduce-scatter.1
